TPU v7x, 32 devices: a whole 2x2x4 slice. The times are simulated.
32 devices in a mesh: dp: 4 (over z), ctx: 8 (over y, x, core).
Axes of the slice: x: 2, y: 2, z: 4, core: 2. Of those that a mesh axis runs over, the one named last changes fastest.
Arguments:
- tokens: bfloat16 [4, 1024, 6144], P('dp', 'ctx'), may hold values from -0.1875 to 0.1875
- cotangent: bfloat16 [4, 1024, 6144], P('dp', 'ctx'), may hold values from -6 to 6
- w_router: float32 [6144], replicated, may hold values from -2 to 2
- w_query: bfloat16 [6144, 4096], P(None, 'ctx'), may hold values from -0.078125 to 0.078125
- w_key: bfloat16 [6144, 4096], P(None, 'ctx'), may hold values from -0.078125 to 0.078125
- w_value: bfloat16 [6144, 4096], P(None, 'ctx'), may hold values from -0.078125 to 0.078125
- w_out: bfloat16 [4096, 6144], P('ctx'), may hold values from -0.09375 to 0.09375
- chosen: int32 [4, 160], P('dp', 'ctx'), may hold values from -1 to 1023, as said below
- counts: int32 [4, 8], P('dp', 'ctx'), may hold values from 12 to 20, as said below
Outputs:
- layer_out: bfloat16 [4, 1024, 6144], P('dp', 'ctx')
- grad_query: bfloat16 [6144, 4096], P('dp', 'ctx')
- grad_key: bfloat16 [6144, 4096], P('dp', 'ctx')
- grad_value: bfloat16 [6144, 4096], P('dp', 'ctx')
- grad_out: bfloat16 [4096, 6144], P('ctx', 'dp')
- grad_router: float32 [6144], replicated
Inputs may be any that keep to these rules, and one draw needn't show every extreme that they name: `chosen`: for every sequence b and device block c, the first counts[b, c] of the block's slots c * 20 to (c + 1) * 20 - 1 hold increasing positions of that device's tokens, c * 128 to (c + 1) * 128 - 1; the other slots hold -1. In every sequence the counts add up to 128, and some device's block has exactly 20 used slots.
All inputs are finite; a program needn't handle non-finite values.
Results may differ from a plain program's by a relative error of at most 0.018.
Values may be sent and summed in bfloat16 or wider, within the bound.
No kernel may reach another device: no remote copies, remote signals or barrier semaphores. Data moves between devices by JAX's collectives and lax.ppermute only.
A program may use at most 128 MiB of HBM per device.

v0:
```python
import math
import jax
import jax.numpy as jnp
from jax import lax
from jax.sharding import PartitionSpec as P

HDIM = 128
HIGHEST_PRECISION = lax.Precision.HIGHEST
ROW_CONTRACT = (((0,), (0,)), ((), ()))
COLUMN_CONTRACT = (((1,), (1,)), ((), ()))


def head_norm(values, width):
    shaped = values.reshape(values.shape[0], -1, width)
    inverse = lax.rsqrt(jnp.mean(shaped * shaped, axis=-1, keepdims=True) + 1e-06)
    return (shaped * inverse, inverse)


def norm_back(grad_hat, normal, inverse):
    return inverse * (grad_hat - normal * jnp.mean(grad_hat * normal, axis=-1, keepdims=True))


def rounded_term(part):
    return lax.optimization_barrier(part.astype(jnp.bfloat16)).astype(jnp.float32)


def body(tokens, cotangent, w_router, w_query, w_key, w_value, w_out, chosen, counts):
    length = tokens.shape[1]
    capacity = chosen.shape[1]
    inner = w_query.shape[1]
    heads_here = inner // HDIM
    scale = 1.0 / math.sqrt(HDIM)
    offset = lax.axis_index("ctx") * length
    slot_ids = lax.broadcasted_iota(jnp.int32, (capacity,), 0)
    local = chosen[0] - offset
    present = (slot_ids < counts[0, 0]) & (local >= 0) & (local < length)
    columns = lax.broadcasted_iota(jnp.int32, (capacity, length), 1)
    onehot = ((local[:, None] == columns) & present[:, None]).astype(jnp.bfloat16)
    rows = jnp.dot(onehot, tokens[0], preferred_element_type=jnp.float32)
    rows_back = jnp.dot(onehot, cotangent[0], preferred_element_type=jnp.float32)
    logits = jnp.dot(rows, w_router, precision=HIGHEST_PRECISION)
    weights = jax.nn.sigmoid(logits)
    normed = (rows * lax.rsqrt(jnp.mean(rows * rows, axis=-1, keepdims=True) + 1e-05)).astype(
        jnp.bfloat16
    )
    delta = (weights[:, None] * rows_back).astype(jnp.bfloat16)
    all_normed, all_delta, all_present = (
        lax.all_gather(normed, "ctx", axis=0, tiled=True),
        lax.all_gather(delta, "ctx", axis=0, tiled=True),
        lax.all_gather(present.astype(jnp.bfloat16), "ctx", axis=0, tiled=True),
    )
    slots = all_normed.shape[0]
    query_raw = jnp.dot(all_normed, w_query, preferred_element_type=jnp.float32)
    key_raw = jnp.dot(all_normed, w_key, preferred_element_type=jnp.float32)
    value_raw = jnp.dot(all_normed, w_value, preferred_element_type=jnp.float32)
    query_hat, query_scale = head_norm(query_raw, HDIM)
    key_hat, key_scale = head_norm(key_raw, HDIM)
    query_b = query_hat.astype(jnp.bfloat16)
    key_b = key_hat.astype(jnp.bfloat16)
    value_b = value_raw.reshape(slots, heads_here, HDIM).astype(jnp.bfloat16)
    current = lax.broadcasted_iota(jnp.int32, (slots, slots), 0)
    earlier = lax.broadcasted_iota(jnp.int32, (slots, slots), 1)
    allowed = (earlier <= current) & ((all_present[None, :] > 0.5) | (earlier == current))
    scores = jnp.einsum("ihd,jhd->hij", query_b, key_b, preferred_element_type=jnp.float32) * scale
    exponent = jnp.where(allowed[None], jnp.exp(scores), 0.0)
    attend = exponent / jnp.sum(exponent, axis=-1, keepdims=True)
    attend_b = attend.astype(jnp.bfloat16)
    mixed = jnp.einsum("hij,jhd->ihd", attend_b, value_b, preferred_element_type=jnp.float32)
    mixed = mixed.astype(jnp.bfloat16).reshape(slots, inner)
    update = lax.psum_scatter(
        rounded_term(jnp.dot(mixed, w_out, preferred_element_type=jnp.float32)).astype(
            jnp.bfloat16
        ),
        "ctx",
        scatter_dimension=0,
        tiled=True,
    ).astype(jnp.float32)
    scaled = weights[:, None] * update
    spread = jnp.dot(onehot.astype(jnp.float32).T, scaled, precision=HIGHEST_PRECISION)
    layer_out = (tokens[0].astype(jnp.float32) + spread).astype(jnp.bfloat16)[None]
    gate_back = jnp.sum(rows_back * update, axis=-1) * weights * (1.0 - weights)
    router_part = jnp.dot(gate_back, rows, precision=HIGHEST_PRECISION)
    grad_router = lax.psum(router_part, ("dp", "ctx"))
    out_term = rounded_term(
        lax.dot_general(mixed, all_delta, ROW_CONTRACT, preferred_element_type=jnp.float32)
    )
    mixed_back = lax.dot_general(
        all_delta, w_out, COLUMN_CONTRACT, preferred_element_type=jnp.float32
    )
    mixed_back = mixed_back.astype(jnp.bfloat16).reshape(slots, heads_here, HDIM)
    attend_back = jnp.einsum(
        "ihd,jhd->hij", mixed_back, value_b, preferred_element_type=jnp.float32
    )
    inner_sum = jnp.sum(attend * attend_back, axis=-1, keepdims=True)
    scores_back = (attend * (attend_back - inner_sum) * scale).astype(jnp.bfloat16)
    value_back = jnp.einsum(
        "hij,ihd->jhd", attend_b, mixed_back, preferred_element_type=jnp.float32
    )
    value_back = value_back.astype(jnp.bfloat16).reshape(slots, inner)
    qhat_back = jnp.einsum("hij,jhd->ihd", scores_back, key_b, preferred_element_type=jnp.float32)
    khat_back = jnp.einsum("hij,ihd->jhd", scores_back, query_b, preferred_element_type=jnp.float32)
    query_back = (
        norm_back(qhat_back, query_hat, query_scale).astype(jnp.bfloat16).reshape(slots, inner)
    )
    key_back = norm_back(khat_back, key_hat, key_scale).astype(jnp.bfloat16).reshape(slots, inner)
    query_term = rounded_term(
        lax.dot_general(all_normed, query_back, ROW_CONTRACT, preferred_element_type=jnp.float32)
    )
    key_term = rounded_term(
        lax.dot_general(all_normed, key_back, ROW_CONTRACT, preferred_element_type=jnp.float32)
    )
    value_term = rounded_term(
        lax.dot_general(all_normed, value_back, ROW_CONTRACT, preferred_element_type=jnp.float32)
    )
    grad_query, grad_key, grad_value, grad_out = (
        lax.psum_scatter(
            query_term.astype(jnp.bfloat16), "dp", scatter_dimension=0, tiled=True
        ).astype(jnp.float32),
        lax.psum_scatter(
            key_term.astype(jnp.bfloat16), "dp", scatter_dimension=0, tiled=True
        ).astype(jnp.float32),
        lax.psum_scatter(
            value_term.astype(jnp.bfloat16), "dp", scatter_dimension=0, tiled=True
        ).astype(jnp.float32),
        lax.psum_scatter(
            out_term.astype(jnp.bfloat16), "dp", scatter_dimension=1, tiled=True
        ).astype(jnp.float32),
    )
    return (
        layer_out,
        grad_query.astype(jnp.bfloat16),
        grad_key.astype(jnp.bfloat16),
        grad_value.astype(jnp.bfloat16),
        grad_out.astype(jnp.bfloat16),
        grad_router,
    )


def solution(mesh):
    in_specs = (
        P("dp", "ctx", None),
        P("dp", "ctx", None),
        P(),
        P(None, "ctx"),
        P(None, "ctx"),
        P(None, "ctx"),
        P("ctx", None),
        P("dp", "ctx"),
        P("dp", "ctx"),
    )
    out_specs = (
        P("dp", "ctx", None),
        P("dp", "ctx"),
        P("dp", "ctx"),
        P("dp", "ctx"),
        P("ctx", "dp"),
        P(),
    )
    return jax.shard_map(body, mesh=mesh, in_specs=in_specs, out_specs=out_specs, check_vma=False)
```

profile of v0, /device:TPU:0, one launch (start us, length us, event | category | flops | bytes accessed | tf_op | source)
XLA Modules:
  0.0 630.2 jit_solution(3186163892697100419)
XLA Ops:
  8.0 0.7 fusion.88
  8.7 1.9 multiply_reduce_fusion.1
  10.6 0.9 fusion.31
  11.6 0.7 fusion.89
  13.1 15.3 %all-reduce = bf16[160]{0:T(256)(128)(2,1)S(1)} all-reduce(bf16[160]{0:T(256)(128)(2,1)S(1)} %dynamic-update-slice), channel_id=1, replica_groups=mesh['dp'=4,'ctx'=8] {'ctx'}, use_global_device_ids=true, to_apply=%add | all-reduce | flops 160 | bytes 640
  28.4 0.7 fusion.54
  29.2 14.3 %all-gather.5.cloned.1.call-done = bf16[8,20,6144]{2,1,0:T(8,128)(2,1)} async-done(((bf16[1,20,6144]{2,1,0:T(8,128)(2,1)}), bf16[8,20,6144]{2,1,0:T(8,128)(2,1)}) %all-gather.5.cloned.1.call-update) | async-done | bytes 1966096 | tf_op jit(solution)/shard_map/all_gather | solution.py:48
  43.4 2.6 reshape.127
  46.0 4.8 fusion.16
  50.8 4.8 fusion.103
  55.7 1.9 fusion.102
  57.6 1.8 reshape.116
  59.4 1.9 multiply_reduce_fusion.5
  61.3 1.0 copy.67
  62.2 1.8 reshape.117
  64.0 1.9 multiply_reduce_fusion.4
  65.9 1.0 copy.69
  66.9 2.4 fusion.28
  69.2 1.5 fusion.14
  70.8 0.6 copy-done.7
  71.4 5.4 convolution_convert_fusion.4
  76.8 30.2 %fusion = bf16[24,6144]{1,0:T(8,128)(2,1)} fusion(bf16[160,6144]{1,0:T(8,128)(2,1)} %convolution_convert_fusion.4), kind=kCustom, calls=%all-reduce-scatter | all-reduce-scatter fusion | flops 1179649 | bytes 2261504
  106.9 2.0 collective-permute-start
  108.9 1.5 slice
  110.5 3.2 collective-permute-start.1
  113.7 2.3 fusion.21
  116.6 9.6 %concatenate = bf16[52,6144]{1,0:T(8,128)(2,1)} concatenate(bf16[4,6144]{1,0:T(4,128)(2,1)} %collective-permute-done.1, bf16[24,6144]{1,0:T(8,128)(2,1)} %collective-permute-done, bf16[24,6144]{1,0:T(8,128)(2,1)} %fusion), dimensions={0} | concatenate | bytes 1277952
  126.2 2.8 fusion.26
  129.1 30.2 %all-gather.7.cloned.1.call-done = bf16[8,20,6144]{2,1,0:T(8,128)(2,1)} async-done(((bf16[1,20,6144]{2,1,0:T(8,128)(2,1)}), bf16[8,20,6144]{2,1,0:T(8,128)(2,1)}) %all-gather.7.cloned.1.call-update) | async-done | bytes 1966096 | tf_op jit(solution)/shard_map/all_gather | solution.py:49
  159.3 4.0 reshape.129
  163.3 6.0 convolution_convert_fusion
  169.6 5.8 fusion.17
  175.4 0.7 copy-done.10
  176.1 1.1 fusion.48
  177.2 2.6 multiply_reduce_fusion.3
  179.8 5.7 convolution_convert_fusion.3
  185.6 2.4 multiply_reduce_fusion.2
  188.0 5.6 convolution_convert_fusion.2
  193.6 0.8 copy-done.11
  194.7 4.4 convolution_convert_fusion.1
  199.2 1.0 copy-done.3
  200.2 0.4 fusion.77
  200.6 47.0 %psum.7 = f32[6144]{0:T(1024)} all-reduce(f32[6144]{0:T(1024)S(1)} %bitcast.169), channel_id=1, replica_groups=mesh['dp'=4,'ctx'=8] {'dp','ctx'}, use_global_device_ids=true, to_apply=%region_13.14 | all-reduce | flops 6144 | bytes 49152 | tf_op jit(solution)/shard_map/psum | solution.py:83
  247.6 4.4 fusion.3
  252.0 29.3 %reduce-scatter.13.cloned.1.call-done = bf16[512,1536]{1,0:T(8,128)(2,1)} async-done(((bf16[512,6144]{1,0:T(8,128)(2,1)}), bf16[512,1536]{1,0:T(8,128)(2,1)}) %reduce-scatter.13.cloned.1.call-update) | async-done | bytes 1572880 | tf_op jit(solution)/shard_map/reduce_scatter | solution.py:125
  281.3 114.0 %reduce-scatter.7.cloned.1.call-done = bf16[1536,512]{1,0:T(8,128)(2,1)} async-done(((bf16[6144,512]{1,0:T(8,128)(2,1)}), bf16[1536,512]{1,0:T(8,128)(2,1)}) %reduce-scatter.7.cloned.1.call-update) | async-done | bytes 1572880 | tf_op jit(solution)/shard_map/reduce_scatter | solution.py:116
  395.3 114.0 %reduce-scatter.9.cloned.1.call-done = bf16[1536,512]{1,0:T(8,128)(2,1)} async-done(((bf16[6144,512]{1,0:T(8,128)(2,1)}), bf16[1536,512]{1,0:T(8,128)(2,1)}) %reduce-scatter.9.cloned.1.call-update) | async-done | bytes 1572880 | tf_op jit(solution)/shard_map/reduce_scatter | solution.py:119
  509.3 114.0 %reduce-scatter.11.cloned.1.call-done = bf16[1536,512]{1,0:T(8,128)(2,1)} async-done(((bf16[6144,512]{1,0:T(8,128)(2,1)}), bf16[1536,512]{1,0:T(8,128)(2,1)}) %reduce-scatter.11.cloned.1.call-update) | async-done | bytes 1572880 | tf_op jit(solution)/shard_map/reduce_scatter | solution.py:122
  (61 shorter events, 1.1 us)
Async XLA Ops:
  7.2 119.0 %copy-start = (bf16[1,128,6144]{2,1,0:T(8,128)(2,1)S(1)}, bf16[1,128,6144]{2,1,0:T(8,128)(2,1)}, u32[]{:S(2)}) copy-start(bf16[1,128,6144]{2,1,0:T(8,128)(2,1)} %param.10) | copy-start | bytes 4718596
  7.2 4.4 copy-start.18
  7.2 36.2 %all-gather.5.cloned.1.call-start = ((), (), s32[]{:S(2)}) async-start(), calls=%async_computation.8 | async-start | bytes 2654208 | tf_op jit(solution)/shard_map/all_gather | solution.py:48
  8.7 20.5 %copy-start.12 = (pred[20]{0:T(512)(128)(4,1)}, pred[20]{0:T(512)(128)(4,1)S(1)}, u32[]{:S(2)}) copy-start(pred[20]{0:T(512)(128)(4,1)S(1)} %get-tuple-element.7) | copy-start | bytes 64
  8.7 20.5 %copy-start.14 = (s32[20]{0:T(128)}, s32[20]{0:T(128)S(1)}, u32[]{:S(2)}) copy-start(s32[20]{0:T(128)S(1)} %get-tuple-element.8) | copy-start | bytes 244
  10.6 18.6 %copy-start.2 = (f32[20,6144]{1,0:T(8,128)}, f32[20,6144]{1,0:T(8,128)S(1)}, u32[]{:S(2)}) copy-start(f32[20,6144]{1,0:T(8,128)S(1)} %get-tuple-element.14) | copy-start | bytes 1474564
  11.5 147.8 %all-gather.7.cloned.1.call-start = ((), (), s32[]{:S(2)}) async-start(), calls=%async_computation.9 | async-start | bytes 2654208 | tf_op jit(solution)/shard_map/all_gather | solution.py:49
  46.0 9.6 %slice-start = ((s8[6291456]{0:T(1024)(128)(4,1)}), s8[4194304]{0:T(1024)(128)(4,1)S(1)}, s32[]{:S(2)}) async-start(s8[6291456]{0:T(1024)(128)(4,1)} %bitcast.167), calls=%async_computation.10 | async-start | bytes 8388608
  50.8 4.8 slice-start.1
  70.7 0.7 copy-start.7
  76.8 49.5 %copy-start.13 = (pred[20]{0:T(512)(128)(4,1)S(1)}, pred[20]{0:T(512)(128)(4,1)}, u32[]{:S(2)}) copy-start(pred[20]{0:T(512)(128)(4,1)} %copy-done.12) | copy-start | bytes 64
  76.8 49.5 %copy-start.15 = (s32[20]{0:T(128)S(1)}, s32[20]{0:T(128)}, u32[]{:S(2)}) copy-start(s32[20]{0:T(128)} %copy-done.14) | copy-start | bytes 244
  106.9 9.7 %collective-permute-start = (bf16[24,6144]{1,0:T(8,128)(2,1)}, bf16[24,6144]{1,0:T(8,128)(2,1)}, u32[]{:S(2)}, u32[]{:S(2)}) collective-permute-start(bf16[24,6144]{1,0:T(8,128)(2,1)} %fusion), channel_id=1, source_target_pairs={{0,1},{1,2},{2,3},{3,4},{4,5},{5,6},{6,7},{8,9},{9,10},{10,11},{11... | collective-permute-start | bytes 884744
  110.5 6.2 collective-permute-start.1
  129.0 34.3 %copy-start.8 = (bf16[4,20,8,128]{3,2,1,0:T(8,128)(2,1)S(1)}, bf16[4,20,8,128]{3,2,1,0:T(8,128)(2,1)}, u32[]{:S(2)}) copy-start(bf16[4,20,8,128]{3,2,1,0:T(8,128)(2,1)} %copy-done.7) | copy-start | bytes 491524
  129.1 152.3 %reduce-scatter.13.cloned.1.call-start = ((), (), s32[]{:S(2)}) async-start(), calls=%async_computation.7 | async-start | bytes 7864320 | tf_op jit(solution)/shard_map/reduce_scatter | solution.py:125
  169.4 6.8 %copy-start.9 = (bf16[20,4,8,128]{3,2,1,0:T(8,128)(2,1)S(1)}, bf16[20,4,8,128]{3,2,1,0:T(8,128)(2,1)}, u32[]{:S(2)}) copy-start(bf16[20,4,8,128]{3,2,1,0:T(8,128)(2,1)} %fusion.16) | copy-start | bytes 491524
  169.4 7.8 %copy-start.4 = (f32[160,512]{1,0:T(8,128)S(1)}, f32[160,512]{1,0:T(8,128)}, u32[]{:S(2)}) copy-start(f32[160,512]{1,0:T(8,128)} %fusion.103) | copy-start | bytes 983044
  169.4 7.8 %copy-start.5 = (f32[160,512]{1,0:T(8,128)S(1)}, f32[160,512]{1,0:T(8,128)}, u32[]{:S(2)}) copy-start(f32[160,512]{1,0:T(8,128)} %fusion.102) | copy-start | bytes 983044
  169.4 7.8 %copy-start.6 = (f32[4,160,160]{1,2,0:T(8,128)S(1)}, f32[4,160,160]{1,2,0:T(8,128)}, u32[]{:S(2)}) copy-start(f32[4,160,160]{1,2,0:T(8,128)} %fusion.28) | copy-start | bytes 1228804
  169.4 225.9 %reduce-scatter.7.cloned.1.call-start = ((), (), s32[]{:S(2)}) async-start(), calls=%async_computation.4 | async-start | bytes 7864320 | tf_op jit(solution)/shard_map/reduce_scatter | solution.py:116
  175.4 0.7 copy-start.10
  185.5 323.8 %reduce-scatter.9.cloned.1.call-start = ((), (), s32[]{:S(2)}) async-start(), calls=%async_computation.5 | async-start | bytes 7864320 | tf_op jit(solution)/shard_map/reduce_scatter | solution.py:119
  193.5 0.9 copy-start.11
  193.6 429.8 %reduce-scatter.11.cloned.1.call-start = ((), (), s32[]{:S(2)}) async-start(), calls=%async_computation.6 | async-start | bytes 7864320 | tf_op jit(solution)/shard_map/reduce_scatter | solution.py:122
  199.1 1.1 copy-start.3
  199.1 1.1 copy-start.16
  199.1 1.1 copy-start.17
  199.2 424.2 %copy-start.1 = (bf16[1,128,6144]{2,1,0:T(8,128)(2,1)S(1)}, bf16[1,128,6144]{2,1,0:T(8,128)(2,1)}, u32[]{:S(2)}) copy-start(bf16[1,128,6144]{2,1,0:T(8,128)(2,1)} %param.10) | copy-start | bytes 4718596
Sparse Core Ops, SparseCore 0:
  11.6 31.7 all-gather.4
  129.2 30.0 all-gather.6
  169.5 111.7 reduce-scatter.12
  284.1 111.2 reduce-scatter.6
  398.0 111.2 reduce-scatter.8
  512.1 111.2 reduce-scatter.10
where the time goes:
time: 632 us; the launch traced here: 630 us
  waiting for transfers between devices  416 us (66%)
  blocking collectives  92.5 us (15%)
  matrix products  66.3 us (10%)
  local copies, waits for them, and re-layouts  27.4 us (4%)
  between operations  16.4 us (3%)
    reduce_scatter x1, waiting for transfers between devices, body(): lax.psum_scatter(value_term.astype(jnp.bfloat16), 'dp', scatter_dimension...  114 us
    reduce_scatter x1, waiting for transfers between devices, body(): lax.psum_scatter(key_term.astype(jnp.bfloat16), 'dp', scatter_dimension=0...  114 us
    reduce_scatter x1, waiting for transfers between devices, body(): lax.psum_scatter(query_term.astype(jnp.bfloat16), 'dp', scatter_dimension...  114 us
    psum x1, blocking collectives, body(): grad_router = lax.psum(router_part, ('dp', 'ctx'))  47 us
    unnamed x2, blocking collectives  45.5 us
    all_gather x1, waiting for transfers between devices, body(): lax.all_gather(delta, 'ctx', axis=0, tiled=True)  30.2 us
    reduce_scatter x1, waiting for transfers between devices, body(): lax.psum_scatter(out_term.astype(jnp.bfloat16), 'dp', scatter_dimension=1...  29.3 us
    unnamed x49, local copies, waits for them, and re-layouts  21.9 us
  transfers between devices with their start and end apart: 8, of which 6 were waited for; matrix products, arithmetic and copies ran while one was open for 6% of the time, Pallas kernels for 0%

commit v1 on v0

--- a/solution.py
+++ b/solution.py
@@ -80,7 +80,7 @@
     layer_out = (tokens[0].astype(jnp.float32) + spread).astype(jnp.bfloat16)[None]
     gate_back = jnp.sum(rows_back * update, axis=-1) * weights * (1.0 - weights)
     router_part = jnp.dot(gate_back, rows, precision=HIGHEST_PRECISION)
-    grad_router = lax.psum(router_part, ("dp", "ctx"))
+    grad_router = jnp.sum(lax.all_gather(router_part, ("dp", "ctx")), 0)
     out_term = rounded_term(
         lax.dot_general(mixed, all_delta, ROW_CONTRACT, preferred_element_type=jnp.float32)
     )

time: 632 us -> 635 us (level)
    all_gather x0 -> x1, blocking collectives: none -> 51.3 us  [body(): grad_router = jnp.sum(lax.all_gather(router_part, ('dp', 'ctx')), 0)]
    psum x1 -> x0, blocking collectives: 47 us -> none  [body(): grad_router = lax.psum(router_part, ('dp', 'ctx'))]
    unnamed x49 -> x51, local copies, waits for them, and re-layouts: 21.9 us -> 21.7 us
  transfers between devices with their start and end apart: 8 -> 8, of which waited for: 6 -> 6; matrix products, arithmetic and copies ran while one was open for 6% -> 7% of each run, Pallas kernels for 0% -> 0%
where the time goes in v1:
time: 635 us; the launch traced here: 633 us
  waiting for transfers between devices  412 us (65%)
  blocking collectives  96.8 us (15%)
  matrix products  65.7 us (10%)
  local copies, waits for them, and re-layouts  29.5 us (5%)
  between operations  16.4 us (3%)
  other arithmetic  7.84 us (1%)
    reduce_scatter x1, waiting for transfers between devices, body(): lax.psum_scatter(query_term.astype(jnp.bfloat16), 'dp', scatter_dimension...  114 us
    reduce_scatter x1, waiting for transfers between devices, body(): lax.psum_scatter(value_term.astype(jnp.bfloat16), 'dp', scatter_dimension...  114 us
    reduce_scatter x1, waiting for transfers between devices, body(): lax.psum_scatter(key_term.astype(jnp.bfloat16), 'dp', scatter_dimension=0...  114 us
    all_gather x1, blocking collectives, body(): grad_router = jnp.sum(lax.all_gather(router_part, ('dp', 'ctx')), 0)  51.3 us
    unnamed x2, blocking collectives  45.5 us
    all_gather x1, waiting for transfers between devices, body(): lax.all_gather(delta, 'ctx', axis=0, tiled=True)  30.3 us
    reduce_scatter x1, waiting for transfers between devices, body(): lax.psum_scatter(out_term.astype(jnp.bfloat16), 'dp', scatter_dimension=1...  24.2 us
    unnamed x51, local copies, waits for them, and re-layouts  21.7 us
  transfers between devices with their start and end apart: 8, of which 6 were waited for; matrix products, arithmetic and copies ran while one was open for 7% of the time, Pallas kernels for 0%

profile of v1, /device:TPU:0, one launch (start us, length us, event | category | flops | bytes accessed | tf_op | source)
XLA Modules:
  0.0 633.3 jit_solution(12831897544611512511)
XLA Ops:
  8.0 0.7 fusion.88
  8.7 1.9 multiply_reduce_fusion.1
  10.6 0.9 fusion.31
  13.1 15.3 %all-reduce = bf16[160]{0:T(256)(128)(2,1)S(1)} all-reduce(bf16[160]{0:T(256)(128)(2,1)S(1)} %dynamic-update-slice), channel_id=1, replica_groups=mesh['dp'=4,'ctx'=8] {'ctx'}, use_global_device_ids=true, to_apply=%add | all-reduce | flops 160 | bytes 640
  28.4 0.7 fusion.54
  29.1 14.4 %all-gather.6.cloned.1.call-done = bf16[8,20,6144]{2,1,0:T(8,128)(2,1)} async-done(((bf16[1,20,6144]{2,1,0:T(8,128)(2,1)}), bf16[8,20,6144]{2,1,0:T(8,128)(2,1)}) %all-gather.6.cloned.1.call-update) | async-done | bytes 1966096 | tf_op jit(solution)/shard_map/all_gather | solution.py:48
  43.5 2.6 reshape.128
  46.1 4.8 fusion.16
  50.9 4.8 fusion.103
  55.7 1.9 fusion.102
  57.7 1.8 reshape.116
  59.5 1.9 multiply_reduce_fusion.5
  61.3 1.0 copy.83
  62.3 1.8 reshape.117
  64.1 1.9 multiply_reduce_fusion.4
  66.0 1.0 copy.85
  67.0 2.4 fusion.28
  69.3 1.5 fusion.14
  70.8 0.7 copy-done.8
  71.5 5.3 convolution_convert_fusion.4
  76.8 30.2 %fusion = bf16[24,6144]{1,0:T(8,128)(2,1)} fusion(bf16[160,6144]{1,0:T(8,128)(2,1)} %convolution_convert_fusion.4), kind=kCustom, calls=%all-reduce-scatter | all-reduce-scatter fusion | flops 1179649 | bytes 2261504
  107.0 2.0 collective-permute-start
  109.0 1.5 slice
  110.5 3.2 collective-permute-start.1
  113.7 2.3 fusion.21
  116.6 9.5 %concatenate = bf16[52,6144]{1,0:T(8,128)(2,1)} concatenate(bf16[4,6144]{1,0:T(4,128)(2,1)} %collective-permute-done.1, bf16[24,6144]{1,0:T(8,128)(2,1)} %collective-permute-done, bf16[24,6144]{1,0:T(8,128)(2,1)} %fusion), dimensions={0} | concatenate | bytes 1277952
  126.1 2.8 fusion.26
  129.0 30.3 %all-gather.8.cloned.1.call-done = bf16[8,20,6144]{2,1,0:T(8,128)(2,1)} async-done(((bf16[1,20,6144]{2,1,0:T(8,128)(2,1)}), bf16[8,20,6144]{2,1,0:T(8,128)(2,1)}) %all-gather.8.cloned.1.call-update) | async-done | bytes 1966096 | tf_op jit(solution)/shard_map/all_gather | solution.py:49
  159.3 4.0 reshape.130
  163.3 6.0 convolution_convert_fusion
  169.6 5.8 fusion.17
  175.4 0.7 copy-done.11
  176.1 1.1 fusion.48
  177.2 2.6 multiply_reduce_fusion.3
  179.8 5.6 convolution_convert_fusion.3
  185.5 2.4 multiply_reduce_fusion.2
  187.9 5.6 convolution_convert_fusion.2
  193.5 0.8 copy-done.12
  194.6 4.4 convolution_convert_fusion.1
  199.1 1.0 copy-done.3
  200.5 51.3 %all-gather = f32[196608]{0:T(1024)} all-gather(f32[6144]{0:T(1024)S(1)} %bitcast.169), channel_id=2, replica_groups=mesh['dp'=4,'ctx'=8] {'dp','ctx'}, dimensions={0}, use_global_device_ids=true | all-gather | bytes 811008 | tf_op jit(solution)/shard_map/all_gather | solution.py:83
  251.8 2.3 reshape.123
  254.1 1.8 reduce_sum.89
  255.9 3.8 fusion.3
  259.7 24.2 %reduce-scatter.13.cloned.1.call-done = bf16[512,1536]{1,0:T(8,128)(2,1)} async-done(((bf16[512,6144]{1,0:T(8,128)(2,1)}), bf16[512,1536]{1,0:T(8,128)(2,1)}) %reduce-scatter.13.cloned.1.call-update) | async-done | bytes 1572880 | tf_op jit(solution)/shard_map/reduce_scatter | solution.py:125
  283.9 114.5 %reduce-scatter.7.cloned.1.call-done = bf16[1536,512]{1,0:T(8,128)(2,1)} async-done(((bf16[6144,512]{1,0:T(8,128)(2,1)}), bf16[1536,512]{1,0:T(8,128)(2,1)}) %reduce-scatter.7.cloned.1.call-update) | async-done | bytes 1572880 | tf_op jit(solution)/shard_map/reduce_scatter | solution.py:116
  398.4 114.0 %reduce-scatter.9.cloned.1.call-done = bf16[1536,512]{1,0:T(8,128)(2,1)} async-done(((bf16[6144,512]{1,0:T(8,128)(2,1)}), bf16[1536,512]{1,0:T(8,128)(2,1)}) %reduce-scatter.9.cloned.1.call-update) | async-done | bytes 1572880 | tf_op jit(solution)/shard_map/reduce_scatter | solution.py:119
  512.4 114.0 %reduce-scatter.11.cloned.1.call-done = bf16[1536,512]{1,0:T(8,128)(2,1)} async-done(((bf16[6144,512]{1,0:T(8,128)(2,1)}), bf16[1536,512]{1,0:T(8,128)(2,1)}) %reduce-scatter.11.cloned.1.call-update) | async-done | bytes 1572880 | tf_op jit(solution)/shard_map/reduce_scatter | solution.py:122
  (65 shorter events, 2.1 us)
Async XLA Ops:
  7.2 119.0 %copy-start = (bf16[1,128,6144]{2,1,0:T(8,128)(2,1)S(1)}, bf16[1,128,6144]{2,1,0:T(8,128)(2,1)}, u32[]{:S(2)}) copy-start(bf16[1,128,6144]{2,1,0:T(8,128)(2,1)} %param.10) | copy-start | bytes 4718596
  7.2 4.4 copy-start.19
  7.2 36.3 %all-gather.6.cloned.1.call-start = ((), (), s32[]{:S(2)}) async-start(), calls=%async_computation.8 | async-start | bytes 2654208 | tf_op jit(solution)/shard_map/all_gather | solution.py:48
  8.7 20.4 %copy-start.13 = (pred[20]{0:T(512)(128)(4,1)}, pred[20]{0:T(512)(128)(4,1)S(1)}, u32[]{:S(2)}) copy-start(pred[20]{0:T(512)(128)(4,1)S(1)} %get-tuple-element.7) | copy-start | bytes 64
  8.7 20.4 %copy-start.15 = (s32[20]{0:T(128)}, s32[20]{0:T(128)S(1)}, u32[]{:S(2)}) copy-start(s32[20]{0:T(128)S(1)} %get-tuple-element.8) | copy-start | bytes 244
  10.6 18.5 %copy-start.2 = (f32[20,6144]{1,0:T(8,128)}, f32[20,6144]{1,0:T(8,128)S(1)}, u32[]{:S(2)}) copy-start(f32[20,6144]{1,0:T(8,128)S(1)} %get-tuple-element.14) | copy-start | bytes 1474564
  11.5 147.8 %all-gather.8.cloned.1.call-start = ((), (), s32[]{:S(2)}) async-start(), calls=%async_computation.9 | async-start | bytes 2654208 | tf_op jit(solution)/shard_map/all_gather | solution.py:49
  46.1 9.7 %slice-start = ((s8[6291456]{0:T(1024)(128)(4,1)}), s8[4194304]{0:T(1024)(128)(4,1)S(1)}, s32[]{:S(2)}) async-start(s8[6291456]{0:T(1024)(128)(4,1)} %bitcast.167), calls=%async_computation.10 | async-start | bytes 8388608
  50.9 4.8 slice-start.1
  70.8 0.7 copy-start.8
  76.8 49.3 %copy-start.14 = (pred[20]{0:T(512)(128)(4,1)S(1)}, pred[20]{0:T(512)(128)(4,1)}, u32[]{:S(2)}) copy-start(pred[20]{0:T(512)(128)(4,1)} %copy-done.13) | copy-start | bytes 64
  76.8 49.3 %copy-start.16 = (s32[20]{0:T(128)S(1)}, s32[20]{0:T(128)}, u32[]{:S(2)}) copy-start(s32[20]{0:T(128)} %copy-done.15) | copy-start | bytes 244
  107.0 9.6 %collective-permute-start = (bf16[24,6144]{1,0:T(8,128)(2,1)}, bf16[24,6144]{1,0:T(8,128)(2,1)}, u32[]{:S(2)}, u32[]{:S(2)}) collective-permute-start(bf16[24,6144]{1,0:T(8,128)(2,1)} %fusion), channel_id=1, source_target_pairs={{0,1},{1,2},{2,3},{3,4},{4,5},{5,6},{6,7},{8,9},{9,10},{10,11},{11... | collective-permute-start | bytes 884744
  110.5 6.1 collective-permute-start.1
  128.9 34.3 %copy-start.9 = (bf16[4,20,8,128]{3,2,1,0:T(8,128)(2,1)S(1)}, bf16[4,20,8,128]{3,2,1,0:T(8,128)(2,1)}, u32[]{:S(2)}) copy-start(bf16[4,20,8,128]{3,2,1,0:T(8,128)(2,1)} %copy-done.8) | copy-start | bytes 491524
  129.0 155.0 %reduce-scatter.13.cloned.1.call-start = ((), (), s32[]{:S(2)}) async-start(), calls=%async_computation.7 | async-start | bytes 7864320 | tf_op jit(solution)/shard_map/reduce_scatter | solution.py:125
  169.3 6.7 %copy-start.10 = (bf16[20,4,8,128]{3,2,1,0:T(8,128)(2,1)S(1)}, bf16[20,4,8,128]{3,2,1,0:T(8,128)(2,1)}, u32[]{:S(2)}) copy-start(bf16[20,4,8,128]{3,2,1,0:T(8,128)(2,1)} %fusion.16) | copy-start | bytes 491524
  169.3 7.8 %copy-start.5 = (f32[160,512]{1,0:T(8,128)S(1)}, f32[160,512]{1,0:T(8,128)}, u32[]{:S(2)}) copy-start(f32[160,512]{1,0:T(8,128)} %fusion.103) | copy-start | bytes 983044
  169.3 7.8 %copy-start.6 = (f32[160,512]{1,0:T(8,128)S(1)}, f32[160,512]{1,0:T(8,128)}, u32[]{:S(2)}) copy-start(f32[160,512]{1,0:T(8,128)} %fusion.102) | copy-start | bytes 983044
  169.4 7.8 %copy-start.7 = (f32[4,160,160]{1,2,0:T(8,128)S(1)}, f32[4,160,160]{1,2,0:T(8,128)}, u32[]{:S(2)}) copy-start(f32[4,160,160]{1,2,0:T(8,128)} %fusion.28) | copy-start | bytes 1228804
  169.4 229.0 %reduce-scatter.7.cloned.1.call-start = ((), (), s32[]{:S(2)}) async-start(), calls=%async_computation.4 | async-start | bytes 7864320 | tf_op jit(solution)/shard_map/reduce_scatter | solution.py:116
  175.4 0.7 copy-start.11
  185.4 327.0 %reduce-scatter.9.cloned.1.call-start = ((), (), s32[]{:S(2)}) async-start(), calls=%async_computation.5 | async-start | bytes 7864320 | tf_op jit(solution)/shard_map/reduce_scatter | solution.py:119
  193.5 0.9 copy-start.12
  193.5 432.9 %reduce-scatter.11.cloned.1.call-start = ((), (), s32[]{:S(2)}) async-start(), calls=%async_computation.6 | async-start | bytes 7864320 | tf_op jit(solution)/shard_map/reduce_scatter | solution.py:122
  199.1 1.1 copy-start.3
  199.1 1.1 copy-start.17
  199.1 1.1 copy-start.18
  199.1 56.8 %copy-start.4 = (bf16[1,128,6144]{2,1,0:T(8,128)(2,1)S(1)}, bf16[1,128,6144]{2,1,0:T(8,128)(2,1)}, u32[]{:S(2)}) copy-start(bf16[1,128,6144]{2,1,0:T(8,128)(2,1)} %param.9) | copy-start | bytes 4718596
  251.8 374.6 %copy-start.1 = (bf16[1,128,6144]{2,1,0:T(8,128)(2,1)S(1)}, bf16[1,128,6144]{2,1,0:T(8,128)(2,1)}, u32[]{:S(2)}) copy-start(bf16[1,128,6144]{2,1,0:T(8,128)(2,1)} %param.10) | copy-start | bytes 4718596
Sparse Core Ops, SparseCore 0:
  11.6 31.8 all-gather.5
  129.1 30.1 all-gather.7
  169.4 114.4 reduce-scatter.12
  286.6 111.6 reduce-scatter.6
  401.1 111.2 reduce-scatter.8
  515.1 111.2 reduce-scatter.10
